TPU v7x, 1024 devices: a whole 4x4x32 slice. The times are simulated.
1024 devices in a mesh: sector: 32 (over y, z_hi, core), op: 32 (over z_lo, x).
Axes of the slice: x: 4, y: 4, z: 32 (z_hi: 4, z_lo: 8; z = z_hi * 8 + z_lo), core: 2. Of those that a mesh axis runs over, the one named last changes fastest.
Arguments:
- psi: bfloat16 [32, 512, 512], P('sector', 'op'), may hold values from -6 to 6
- in_sector: int32 [32, 32], P('sector'), may hold values from 0 to 31
- term_count: int32 [32, 32], P('sector', 'op'), may hold values from 1 to 4, as said below
- coef_index: int32 [32, 128], P('sector', 'op'), may hold values from 0 to 63
- left_index: int32 [32, 128], P('sector', 'op'), may hold values from 0 to 1
- term_values: float32 [64], replicated, may hold values from -0.9 to 0.9
- left_ops: bfloat16 [32, 2, 512, 512], P('sector'), may hold values from -0.25 to 0.25
- right_ops: bfloat16 [32, 128, 512, 512], P('sector', 'op'), may hold values from -0.25 to 0.25
Outputs:
- hpsi: float32 [32, 512, 512], P('sector', 'op')
Inputs may be any that keep to these rules, and one draw needn't show every extreme that they name: `term_count`: some device has all 4 slots live in every draw.
All inputs are finite; a program needn't handle non-finite values.
Results may differ from a plain program's by a relative error of at most 0.0029.
Values may be sent and summed in bfloat16 or wider, within the bound.
No kernel may reach another device: no remote copies, remote signals or barrier semaphores. Data moves between devices by JAX's collectives and lax.ppermute only.
A program may use at most 32 MiB of HBM per device.

v0:
```python
import jax
import jax.numpy as jnp
from jax import lax
from jax.sharding import PartitionSpec as P


def body(psi, in_sector, term_count, coef_index, left_index, term_values, left_ops, right_ops):
    ops = lax.axis_size("op")
    slab_rows = psi.shape[1]
    width = psi.shape[2]
    slabs = lax.all_gather(psi, "sector", axis=0, tiled=True)
    wanted = in_sector[0]
    outgoing = jnp.take(slabs, wanted, axis=0)
    arrived = lax.all_to_all(outgoing, "op", split_axis=0, concat_axis=0, tiled=True)
    block = arrived.reshape(ops * slab_rows, width)
    slots = right_ops.shape[1]
    count = term_count[0, 0]
    table_size = term_values.shape[0]
    onehot = (coef_index[0][:, None] == jnp.arange(table_size, dtype=jnp.int32)[None, :]).astype(
        jnp.float32
    )
    weights = jnp.sum(onehot * term_values[None, :], axis=1)
    live = jnp.arange(slots, dtype=jnp.int32) < count
    weights = jnp.where(live, weights, 0.0)
    lefts = [
        lax.dynamic_index_in_dim(left_ops[0], left_index[0, k], 0, keepdims=False)
        for k in range(slots)
    ]
    halves = []
    for k in range(slots):
        halves.append(
            jnp.dot(block, right_ops[0, k], preferred_element_type=jnp.float32).astype(jnp.bfloat16)
        )
    total = jnp.zeros((ops * slab_rows, width), jnp.float32)
    for k in range(slots):
        left_rows = lefts[k]
        total = total + weights[k] * jnp.dot(
            left_rows, halves[k], preferred_element_type=jnp.float32
        )
    mine = lax.psum_scatter(total, "op", scatter_dimension=0, tiled=True)
    return mine.reshape(1, slab_rows, width)


def solution(mesh):
    in_specs = (
        P("sector", "op", None),
        P("sector", None),
        P("sector", "op"),
        P("sector", "op"),
        P("sector", "op"),
        P(),
        P("sector", None, None, None),
        P("sector", "op", None, None),
    )
    out_specs = P("sector", "op", None)
    return jax.shard_map(body, mesh=mesh, in_specs=in_specs, out_specs=out_specs, check_vma=False)
```

profile of v0, /device:TPU:16, one launch (start us, length us, event | category | flops | bytes accessed | tf_op | source)
XLA Modules:
  0.0 394.2 jit_solution(16563683586271740271)
XLA Ops:
  6.5 0.0 copy-start
  6.5 0.0 copy-start.2
  6.5 0.0 copy-start.3
  6.5 0.7 fusion.31
  7.3 0.7 compare_and_fusion
  8.0 83.3 %all_gather.3 = bf16[32,16,512]{2,1,0:T(8,128)(2,1)S(1)} all-gather(bf16[1,16,512]{2,1,0:T(8,128)(2,1)} %param.8), channel_id=1, replica_groups=mesh['sector'=32,'op'=32] {'sector'}, dimensions={0}, use_global_device_ids=true | all-gather | bytes 540672 | tf_op jit(solution)/shard_map/all_gather | solution.py:11
  91.3 0.6 gather_fusion
  91.9 0.9 broadcast_select_fusion
  92.8 9.4 %all-to-all-start = ((bf16[32,16,512]{2,1,0:T(8,128)(2,1)}), bf16[32,16,512]{2,1,0:T(8,128)(2,1)S(1)}, u32[]{:S(2)}, u32[]{:S(2)}) async-start(bf16[32,16,512]{2,1,0:T(8,128)(2,1)} %broadcast_select_fusion), calls=%async_computation | async-start | bytes 1048576 | tf_op jit(solution)/shard_map/all_to_all | solution.py:14
  102.2 0.0 reduce-scatter.2.cloned.1.call-start
  102.3 0.0 copy-done.1
  102.3 0.7 fusion.33
  111.1 0.0 copy-done.2
  111.1 0.0 copy-done.3
  111.1 0.2 select_reduce_fusion
  111.3 0.7 fusion.32
  112.0 20.4 %all-to-all-done = bf16[32,16,512]{2,1,0:T(8,128)(2,1)S(1)} async-done(((bf16[32,16,512]{2,1,0:T(8,128)(2,1)}), bf16[32,16,512]{2,1,0:T(8,128)(2,1)S(1)}, u32[]{:S(2)}, u32[]{:S(2)}) %all-to-all-start) | async-done | bytes 524320 | tf_op jit(solution)/shard_map/all_to_all | solution.py:14
  132.4 0.0 copy-done
  132.4 2.5 convolution_multiply_fusion.3
  134.9 3.4 fusion.2
  138.3 2.8 fusion.1
  141.1 3.4 fusion
  144.5 0.0 reduce-scatter.2.cloned.1.call-update
  144.6 242.8 %reduce-scatter.2.cloned.1.call-done = f32[16,512]{1,0:T(8,128)} async-done(((f32[512,512]{1,0:T(8,128)}), f32[16,512]{1,0:T(8,128)}) %reduce-scatter.2.cloned.1.call-update) | async-done | bytes 32784 | tf_op jit(solution)/shard_map/reduce_scatter | solution.py:40
  (3 shorter events, 0.0 us)
Async XLA Ops:
  6.5 125.8 %copy-start = (bf16[1,2,512,512]{3,2,1,0:T(8,128)(2,1)S(1)}, bf16[1,2,512,512]{3,2,1,0:T(8,128)(2,1)}, u32[]{:S(2)}) copy-start(bf16[1,2,512,512]{3,2,1,0:T(8,128)(2,1)} %param.14) | copy-start | bytes 3145732
  6.5 95.7 %copy-start.1 = (s32[1,4]{1,0:T(1,128)S(1)}, s32[1,4]{1,0:T(1,128)}, u32[]{:S(2)}) copy-start(s32[1,4]{1,0:T(1,128)} %param.12) | copy-start | bytes 52
  6.5 104.6 %copy-start.2 = (f32[64]{0:T(128)S(1)}, f32[64]{0:T(128)}, u32[]{:S(2)}) copy-start(f32[64]{0:T(128)} %param.13) | copy-start | bytes 772
  6.5 104.6 %copy-start.3 = (s32[1,4]{1,0:T(1,128)S(1)}, s32[1,4]{1,0:T(1,128)}, u32[]{:S(2)}) copy-start(s32[1,4]{1,0:T(1,128)} %param.11) | copy-start | bytes 52
  92.8 39.6 %all-to-all-start = ((bf16[32,16,512]{2,1,0:T(8,128)(2,1)}), bf16[32,16,512]{2,1,0:T(8,128)(2,1)S(1)}, u32[]{:S(2)}, u32[]{:S(2)}) async-start(bf16[32,16,512]{2,1,0:T(8,128)(2,1)} %broadcast_select_fusion), calls=%async_computation | async-start | bytes 1048576 | tf_op jit(solution)/shard_map/all_to_all | solution.py:14
  102.2 285.1 %reduce-scatter.2.cloned.1.call-start = ((), (), s32[]{:S(2)}) async-start(), calls=%async_computation.2 | async-start | bytes 1081344 | tf_op jit(solution)/shard_map/reduce_scatter | solution.py:40
Sparse Core Ops, SparseCore 0:
  144.7 242.5 reduce-scatter.1
where the time goes:
time: 395 us; the launch traced here: 394 us
  waiting for transfers between devices  263 us (67%)
  blocking collectives  83.3 us (21%)
  between operations  21.7 us (5%)
  matrix products  12.2 us (3%)
  starting transfers between devices  9.47 us (2%)
    reduce_scatter x1, waiting for transfers between devices, body(): mine = lax.psum_scatter(total, 'op', scatter_dimension=0, tiled=True)  243 us
    all_gather x1, blocking collectives, body(): slabs = lax.all_gather(psi, 'sector', axis=0, tiled=True)  83.3 us
    all_to_all x1, waiting for transfers between devices, body(): lax.all_to_all(outgoing, 'op', split_axis=0, concat_axis=0, tiled=True)  20.4 us
    dot_general x4, matrix products, body(): jnp.dot(left_rows, halves[k], preferred_element_type=jnp.float32)  12.2 us
    all_to_all x1, starting transfers between devices, body(): lax.all_to_all(outgoing, 'op', split_axis=0, concat_axis=0, tiled=True)  9.43 us
  transfers between devices with their start and end apart: 2, of which 2 were waited for; matrix products, arithmetic and copies ran while one was open for 0% of the time, Pallas kernels for 0%

commit v1 on v0

v1 whole, which is shorter than its diff:
```python
import jax
import jax.numpy as jnp
import numpy as np
from jax import lax
from jax.sharding import Mesh, PartitionSpec as P

GATHER = "h_czy"
REDUCE = "h_a2a"

SEC = ("y", "zh", "c")
OPX = ("zl", "x")


def gather_psi(psi):
    if GATHER == "ag":
        g = lax.all_gather(psi, SEC, axis=0, tiled=True)
        return g, lambda s: s
    if GATHER == "h_cyz":
        g = lax.all_gather(psi, "c", axis=0, tiled=True)
        g = lax.all_gather(g, "y", axis=0, tiled=True)
        g = lax.all_gather(g, "zh", axis=0, tiled=True)
        return g, lambda s: (s % 8) // 2 * 8 + s // 8 * 2 + s % 2
    if GATHER == "h_czy":
        g = lax.all_gather(psi, "c", axis=0, tiled=True)
        g = lax.all_gather(g, "zh", axis=0, tiled=True)
        g = lax.all_gather(g, "y", axis=0, tiled=True)
        return g, lambda s: s
    if GATHER == "a2a":
        n = 32
        rep = jnp.broadcast_to(psi, (n,) + psi.shape[1:])
        g = lax.all_to_all(rep, SEC, split_axis=0, concat_axis=0, tiled=True)
        return g, lambda s: s
    raise ValueError


def reduce_out(total, slab_rows, width):
    if REDUCE == "rs":
        return lax.psum_scatter(total, OPX, scatter_dimension=0, tiled=True)
    if REDUCE == "a2a":
        parts = lax.all_to_all(total.reshape(32, slab_rows, width), OPX, split_axis=0, concat_axis=0, tiled=True)
        return jnp.sum(parts, axis=0)
    if REDUCE == "h_rs":
        t = total.reshape(8, 4, slab_rows, width).transpose(1, 0, 2, 3)
        t = lax.psum_scatter(t, "x", scatter_dimension=0, tiled=True)
        t = lax.psum_scatter(t.reshape(8, slab_rows, width), "zl", scatter_dimension=0, tiled=True)
        return t
    if REDUCE == "h_a2a":
        t = total.reshape(8, 4, slab_rows, width).transpose(1, 0, 2, 3)
        t = lax.all_to_all(t, "x", split_axis=0, concat_axis=0, tiled=True)
        t = jnp.sum(t, axis=0)
        t = lax.all_to_all(t, "zl", split_axis=0, concat_axis=0, tiled=True)
        return jnp.sum(t, axis=0)
    if REDUCE == "h_rs_a2a":
        t = total.reshape(8, 4, slab_rows, width).transpose(1, 0, 2, 3)
        t = lax.psum_scatter(t, "x", scatter_dimension=0, tiled=True).reshape(8, slab_rows, width)
        t = lax.all_to_all(t, "zl", split_axis=0, concat_axis=0, tiled=True)
        return jnp.sum(t, axis=0)
    if REDUCE == "h_a2a_rs":
        t = total.reshape(8, 4, slab_rows, width).transpose(1, 0, 2, 3)
        t = lax.all_to_all(t, "x", split_axis=0, concat_axis=0, tiled=True)
        t = jnp.sum(t, axis=0)
        return lax.psum_scatter(t, "zl", scatter_dimension=0, tiled=True)
    raise ValueError


def body(psi, in_sector, term_count, coef_index, left_index, term_values, left_ops, right_ops):
    ops = 32
    slab_rows = psi.shape[1]
    width = psi.shape[2]
    slabs, remap = gather_psi(psi)
    wanted = remap(in_sector[0])
    outgoing = jnp.take(slabs, wanted, axis=0)
    arrived = lax.all_to_all(outgoing, OPX, split_axis=0, concat_axis=0, tiled=True)
    block = arrived.reshape(ops * slab_rows, width)
    slots = right_ops.shape[1]
    count = term_count[0, 0]
    table_size = term_values.shape[0]
    onehot = (coef_index[0][:, None] == jnp.arange(table_size, dtype=jnp.int32)[None, :]).astype(jnp.float32)
    weights = jnp.sum(onehot * term_values[None, :], axis=1)
    live = jnp.arange(slots, dtype=jnp.int32) < count
    weights = jnp.where(live, weights, 0.0)
    lefts = [lax.dynamic_index_in_dim(left_ops[0], left_index[0, k], 0, keepdims=False) for k in range(slots)]
    halves = [jnp.dot(block, right_ops[0, k], preferred_element_type=jnp.float32).astype(jnp.bfloat16) for k in range(slots)]
    total = jnp.zeros((ops * slab_rows, width), jnp.float32)
    for k in range(slots):
        total = total + weights[k] * jnp.dot(lefts[k], halves[k], preferred_element_type=jnp.float32)
    mine = reduce_out(total, slab_rows, width)
    return mine.reshape(1, slab_rows, width)


def solution(mesh):
    devs = np.asarray(mesh.devices).reshape(4, 4, 2, 8, 4)
    fine = Mesh(devs, ("y", "zh", "c", "zl", "x"))
    in_specs = (
        P(SEC, OPX, None),
        P(SEC, None),
        P(SEC, OPX),
        P(SEC, OPX),
        P(SEC, OPX),
        P(),
        P(SEC, None, None, None),
        P(SEC, OPX, None, None),
    )
    out_specs = P(SEC, OPX, None)
    return jax.shard_map(body, mesh=fine, in_specs=in_specs, out_specs=out_specs, check_vma=False)
```

time: 395 us -> 145 us (0.37)
  the two profiles are of different devices: /device:TPU:16 before, /device:TPU:8 now
where the time goes in v1:
time: 145 us
  blocking collectives  96 us (66%)
  waiting for transfers between devices  15.5 us (11%)
  matrix products  12.5 us (9%)
  between operations  8.37 us (6%)
  starting transfers between devices  6.97 us (5%)
  other arithmetic  3.23 us (2%)
  local copies, waits for them, and re-layouts  2 us (1%)
    all_gather x1, blocking collectives, gather_psi(): g = lax.all_gather(g, 'zh', axis=0, tiled=True)  45 us
    all_to_all x1, blocking collectives, reduce_out(): t = lax.all_to_all(t, 'zl', split_axis=0, concat_axis=0, tiled=True)  21.6 us
    all_to_all x1, waiting for transfers between devices, body(): lax.all_to_all(outgoing, OPX, split_axis=0, concat_axis=0, tiled=True)  15.5 us
    all_to_all x1, blocking collectives, reduce_out(): t = lax.all_to_all(t, 'x', split_axis=0, concat_axis=0, tiled=True)  14.4 us
    all_gather x1, blocking collectives, gather_psi(): g = lax.all_gather(g, 'y', axis=0, tiled=True)  13 us
    dot_general x4, matrix products, body(): jnp.dot(lefts[k], halves[k], preferred_element_type=jnp.float32)  12.5 us
    all_to_all x1, starting transfers between devices, body(): lax.all_to_all(outgoing, OPX, split_axis=0, concat_axis=0, tiled=True)  6.97 us
  transfers between devices with their start and end apart: 1, of which 1 were waited for; matrix products, arithmetic and copies ran while one was open for 1% of the time, Pallas kernels for 0%

profile of v1, /device:TPU:8, one launch (start us, length us, event | category | flops | bytes accessed | tf_op | source)
XLA Modules:
  0.0 144.5 jit_solution(4249024719637964289)
XLA Ops:
  0.0 0.0 copy-start
  0.0 0.0 copy-start.3
  0.0 0.7 fusion.31
  0.8 0.7 compare_and_fusion
  1.4 2.0 %all_gather.9 = bf16[2,16,512]{2,1,0:T(8,128)(2,1)S(1)} all-gather(bf16[1,16,512]{2,1,0:T(8,128)(2,1)} %param.8), channel_id=1, replica_groups=mesh['y'=4,'zh'=4,'c'=2,'zl'=8,'x'=4] {'c'}, dimensions={0}, use_global_device_ids=true | all-gather | bytes 49152 | tf_op jit(solution)/shard_map/all_gather | solution.py:24
  3.5 45.0 %all_gather.10 = bf16[8,16,512]{2,1,0:T(8,128)(2,1)S(1)} all-gather(bf16[2,16,512]{2,1,0:T(8,128)(2,1)S(1)} %all_gather.9), channel_id=1, replica_groups=mesh['y'=4,'zh'=4,'c'=2,'zl'=8,'x'=4] {'zh'}, dimensions={0}, use_global_device_ids=true | all-gather | bytes 163840 | tf_op jit(solution)/shard_map/all_gather | solution.py:25
  48.4 13.0 %all_gather.11 = bf16[32,16,512]{2,1,0:T(8,128)(2,1)S(1)} all-gather(bf16[8,16,512]{2,1,0:T(8,128)(2,1)S(1)} %all_gather.10), channel_id=1, replica_groups=mesh['y'=4,'zh'=4,'c'=2,'zl'=8,'x'=4] {'y'}, dimensions={0}, use_global_device_ids=true | all-gather | bytes 655360 | tf_op jit(solution)/shard_map/all_gather | solution.py:26
  61.4 0.6 gather_fusion
  62.0 0.9 broadcast_select_fusion
  62.9 7.0 %all-to-all-start = ((bf16[32,16,512]{2,1,0:T(8,128)(2,1)}), bf16[32,16,512]{2,1,0:T(8,128)(2,1)S(1)}, u32[]{:S(2)}, u32[]{:S(2)}) async-start(bf16[32,16,512]{2,1,0:T(8,128)(2,1)} %broadcast_select_fusion), calls=%async_computation | async-start | bytes 1048576 | tf_op jit(solution)/shard_map/all_to_all | solution.py:73
  69.9 0.0 copy-done.1
  69.9 0.7 fusion.33
  78.9 0.2 select_reduce_fusion
  79.1 0.7 fusion.32
  79.7 15.5 %all-to-all-done = bf16[32,16,512]{2,1,0:T(8,128)(2,1)S(1)} async-done(((bf16[32,16,512]{2,1,0:T(8,128)(2,1)}), bf16[32,16,512]{2,1,0:T(8,128)(2,1)S(1)}, u32[]{:S(2)}, u32[]{:S(2)}) %all-to-all-start) | async-done | bytes 524320 | tf_op jit(solution)/shard_map/all_to_all | solution.py:73
  95.2 3.5 %convolution_multiply_fusion.3 = f32[512,512]{1,0:T(8,128)} fusion(bf16[512,512]{1,0:T(8,128)(2,1)S(1)} %bitcast.55, bf16[1,4,512,512]{3,2,1,0:T(8,128)(2,1)} %param.15, bf16[1,2,512,512]{3,2,1,0:T(8,128)(2,1)S(1)} %copy-done, s32[]{:T(128)S(6)} %select_n.38, f32[]{:T(128)} %bitcast.2), kind=kOutput, calls=%fused_computation.7 | convolution fusion | flops 537395200 | bytes 2621956 | tf_op jit(solution)/shard_map/dot_general | solution.py:86
  98.7 2.7 %fusion.2 = f32[512,512]{1,0:T(8,128)S(1)} fusion(f32[512,512]{1,0:T(8,128)} %convolution_multiply_fusion.3, bf16[512,512]{1,0:T(8,128)(2,1)S(1)} %bitcast.56, bf16[1,4,512,512]{3,2,1,0:T(8,128)(2,1)} %param.15, bf16[1,2,512,512]{3,2,1,0:T(8,128)(2,1)S(1)} %copy-done, s32[]{:T(128)S(6)} %select_n.42, f32[]{:T(128)} %bitcast.10), kind=kOutput, calls=%fused_computation.6 | convolution fusion | flops 537657344 | bytes 3670532 | tf_op jit(solution)/shard_map/dot_general | solution.py:86
  101.4 3.5 %fusion.1 = f32[512,512]{1,0:T(8,128)} fusion(f32[512,512]{1,0:T(8,128)S(1)} %fusion.2, bf16[512,512]{1,0:T(8,128)(2,1)S(1)} %bitcast.57, bf16[1,4,512,512]{3,2,1,0:T(8,128)(2,1)} %param.15, bf16[1,2,512,512]{3,2,1,0:T(8,128)(2,1)S(1)} %copy-done, s32[]{:T(128)S(6)} %select_n.43, f32[]{:T(128)} %bitcast.14), kind=kOutput, calls=%fused_computation.4 | convolution fusion | flops 537657344 | bytes 3670532 | tf_op jit(solution)/shard_map/dot_general | solution.py:86
  104.9 2.8 %fusion = f32[512,512]{1,0:T(8,128)S(1)} fusion(f32[512,512]{1,0:T(8,128)} %fusion.1, bf16[512,512]{1,0:T(8,128)(2,1)S(1)} %bitcast.58, bf16[1,4,512,512]{3,2,1,0:T(8,128)(2,1)} %param.15, bf16[1,2,512,512]{3,2,1,0:T(8,128)(2,1)S(1)} %copy-done, s32[]{:T(128)S(6)} %select_n.44, f32[]{:T(128)} %bitcast.18), kind=kOutput, calls=%fused_computation.2 | convolution fusion | flops 537657344 | bytes 3670532 | tf_op jit(solution)/shard_map/dot_general | solution.py:86
  107.7 0.1 copy.12
  107.8 14.4 %all_to_all.15 = f32[4,8,16,512]{3,2,1,0:T(8,128)S(1)} all-to-all(f32[4,8,16,512]{3,2,1,0:T(8,128)S(1)} %bitcast.59), channel_id=1, replica_groups=mesh['y'=4,'zh'=4,'c'=2,'zl'=8,'x'=4] {'x'}, dimensions={0} | all-to-all | bytes 2097152 | tf_op jit(solution)/shard_map/all_to_all | solution.py:49
  122.2 0.1 reduce_sum.28
  122.3 21.6 %all_to_all.16 = f32[8,16,512]{2,1,0:T(8,128)S(1)} all-to-all(f32[8,16,512]{2,1,0:T(8,128)S(1)} %reduce_sum.28), channel_id=1, replica_groups=mesh['y'=4,'zh'=4,'c'=2,'zl'=8,'x'=4] {'zl'}, dimensions={0} | all-to-all | bytes 524288 | tf_op jit(solution)/shard_map/all_to_all | solution.py:51
  143.9 0.6 reduce_sum.29
  (7 shorter events, 0.0 us)
Async XLA Ops:
  0.0 95.2 %copy-start = (bf16[1,2,512,512]{3,2,1,0:T(8,128)(2,1)S(1)}, bf16[1,2,512,512]{3,2,1,0:T(8,128)(2,1)}, u32[]{:S(2)}) copy-start(bf16[1,2,512,512]{3,2,1,0:T(8,128)(2,1)} %param.14) | copy-start | bytes 3145732
  0.0 69.9 %copy-start.1 = (s32[1,4]{1,0:T(1,128)S(1)}, s32[1,4]{1,0:T(1,128)}, u32[]{:S(2)}) copy-start(s32[1,4]{1,0:T(1,128)} %param.12) | copy-start | bytes 52
  0.0 78.9 %copy-start.2 = (f32[64]{0:T(128)S(1)}, f32[64]{0:T(128)}, u32[]{:S(2)}) copy-start(f32[64]{0:T(128)} %param.13) | copy-start | bytes 772
  0.0 78.9 %copy-start.3 = (s32[1,4]{1,0:T(1,128)S(1)}, s32[1,4]{1,0:T(1,128)}, u32[]{:S(2)}) copy-start(s32[1,4]{1,0:T(1,128)} %param.11) | copy-start | bytes 52
  62.9 32.3 %all-to-all-start = ((bf16[32,16,512]{2,1,0:T(8,128)(2,1)}), bf16[32,16,512]{2,1,0:T(8,128)(2,1)S(1)}, u32[]{:S(2)}, u32[]{:S(2)}) async-start(bf16[32,16,512]{2,1,0:T(8,128)(2,1)} %broadcast_select_fusion), calls=%async_computation | async-start | bytes 1048576 | tf_op jit(solution)/shard_map/all_to_all | solution.py:73

commit v2 on v1

--- a/solution.py
+++ b/solution.py
@@ -5,7 +5,9 @@
 from jax.sharding import Mesh, PartitionSpec as P
 
 GATHER = "h_czy"
-REDUCE = "h_a2a"
+REDUCE = "h_a2a_xbf"
+ROUTE = "flat"
+COMPUTE = "batch"
 
 SEC = ("y", "zh", "c")
 OPX = ("zl", "x")
@@ -23,6 +25,34 @@
     if GATHER == "h_czy":
         g = lax.all_gather(psi, "c", axis=0, tiled=True)
         g = lax.all_gather(g, "zh", axis=0, tiled=True)
+        g = lax.all_gather(g, "y", axis=0, tiled=True)
+        return g, lambda s: s
+    if GATHER == "h_zyc":
+        g = lax.all_gather(psi, "zh", axis=0, tiled=True)
+        g = lax.all_gather(g, "y", axis=0, tiled=True)
+        g = lax.all_gather(g, "c", axis=0, tiled=True)
+        return g, lambda s: (s % 2) * 16 + (s // 8) * 4 + (s % 8) // 2
+    if GATHER == "h_yzc":
+        g = lax.all_gather(psi, "y", axis=0, tiled=True)
+        g = lax.all_gather(g, "zh", axis=0, tiled=True)
+        g = lax.all_gather(g, "c", axis=0, tiled=True)
+        return g, lambda s: (s % 2) * 16 + ((s % 8) // 2) * 4 + s // 8
+    if GATHER == "c_yz":
+        g = lax.all_gather(psi, "c", axis=0, tiled=True)
+        g = lax.all_gather(g, ("y", "zh"), axis=0, tiled=True)
+        return g, lambda s: s
+    if GATHER == "c_zpsum_y":
+        g = lax.all_gather(psi, "c", axis=0, tiled=True)
+        zi = lax.axis_index("zh")
+        buf = jnp.zeros((4,) + g.shape, g.dtype)
+        buf = lax.dynamic_update_index_in_dim(buf, g, zi, 0)
+        g = lax.psum(buf, "zh").reshape((8,) + g.shape[1:])
+        g = lax.all_gather(g, "y", axis=0, tiled=True)
+        return g, lambda s: s
+    if GATHER == "c_za2a_y":
+        g = lax.all_gather(psi, "c", axis=0, tiled=True)
+        rep = jnp.broadcast_to(g[None], (4,) + g.shape).reshape((8,) + g.shape[1:])
+        g = lax.all_to_all(rep, "zh", split_axis=0, concat_axis=0, tiled=True)
         g = lax.all_gather(g, "y", axis=0, tiled=True)
         return g, lambda s: s
     if GATHER == "a2a":
@@ -44,6 +74,18 @@
         t = lax.psum_scatter(t, "x", scatter_dimension=0, tiled=True)
         t = lax.psum_scatter(t.reshape(8, slab_rows, width), "zl", scatter_dimension=0, tiled=True)
         return t
+    if REDUCE == "h_a2a_zbf":
+        t = total.reshape(8, 4, slab_rows, width).transpose(1, 0, 2, 3)
+        t = lax.all_to_all(t, "x", split_axis=0, concat_axis=0, tiled=True)
+        t = jnp.sum(t, axis=0).astype(jnp.bfloat16)
+        t = lax.all_to_all(t, "zl", split_axis=0, concat_axis=0, tiled=True)
+        return jnp.sum(t.astype(jnp.float32), axis=0)
+    if REDUCE == "h_a2a_xbf":
+        t = total.reshape(8, 4, slab_rows, width).transpose(1, 0, 2, 3).astype(jnp.bfloat16)
+        t = lax.all_to_all(t, "x", split_axis=0, concat_axis=0, tiled=True)
+        t = jnp.sum(t.astype(jnp.float32), axis=0)
+        t = lax.all_to_all(t, "zl", split_axis=0, concat_axis=0, tiled=True)
+        return jnp.sum(t, axis=0)
     if REDUCE == "h_a2a":
         t = total.reshape(8, 4, slab_rows, width).transpose(1, 0, 2, 3)
         t = lax.all_to_all(t, "x", split_axis=0, concat_axis=0, tiled=True)
@@ -70,7 +112,14 @@
     slabs, remap = gather_psi(psi)
     wanted = remap(in_sector[0])
     outgoing = jnp.take(slabs, wanted, axis=0)
-    arrived = lax.all_to_all(outgoing, OPX, split_axis=0, concat_axis=0, tiled=True)
+    if ROUTE == "flat":
+        arrived = lax.all_to_all(outgoing, OPX, split_axis=0, concat_axis=0, tiled=True)
+    else:
+        t = outgoing.reshape(8, 4, slab_rows, width).transpose(1, 0, 2, 3)
+        t = lax.all_to_all(t, "x", split_axis=0, concat_axis=0, tiled=True)
+        t = t.transpose(1, 0, 2, 3)
+        t = lax.all_to_all(t, "zl", split_axis=0, concat_axis=0, tiled=True)
+        arrived = t.reshape(32, slab_rows, width)
     block = arrived.reshape(ops * slab_rows, width)
     slots = right_ops.shape[1]
     count = term_count[0, 0]
@@ -79,11 +128,17 @@
     weights = jnp.sum(onehot * term_values[None, :], axis=1)
     live = jnp.arange(slots, dtype=jnp.int32) < count
     weights = jnp.where(live, weights, 0.0)
-    lefts = [lax.dynamic_index_in_dim(left_ops[0], left_index[0, k], 0, keepdims=False) for k in range(slots)]
-    halves = [jnp.dot(block, right_ops[0, k], preferred_element_type=jnp.float32).astype(jnp.bfloat16) for k in range(slots)]
-    total = jnp.zeros((ops * slab_rows, width), jnp.float32)
-    for k in range(slots):
-        total = total + weights[k] * jnp.dot(lefts[k], halves[k], preferred_element_type=jnp.float32)
+    if COMPUTE == "loop":
+        lefts = [lax.dynamic_index_in_dim(left_ops[0], left_index[0, k], 0, keepdims=False) for k in range(slots)]
+        halves = [jnp.dot(block, right_ops[0, k], preferred_element_type=jnp.float32).astype(jnp.bfloat16) for k in range(slots)]
+        total = jnp.zeros((ops * slab_rows, width), jnp.float32)
+        for k in range(slots):
+            total = total + weights[k] * jnp.dot(lefts[k], halves[k], preferred_element_type=jnp.float32)
+    else:
+        lefts = jnp.take(left_ops[0], left_index[0], axis=0)
+        halves = jnp.einsum("ij,kjl->kil", block, right_ops[0], preferred_element_type=jnp.float32).astype(jnp.bfloat16)
+        prods = jnp.einsum("kij,kjl->kil", lefts, halves, preferred_element_type=jnp.float32)
+        total = jnp.sum(weights[:, None, None] * prods, axis=0)
     mine = reduce_out(total, slab_rows, width)
     return mine.reshape(1, slab_rows, width)
 

time: 145 us -> 135 us (0.931)
  matrix products: 12.5 us -> 4.08 us
  between operations: 8.37 us -> 0.75 us
  waiting for transfers between devices: 15.5 us -> 22.2 us
  blocking collectives: 96 us -> 91.1 us
  local copies, waits for them, and re-layouts: 2 us -> 4.52 us
    dot_general x4 -> x1, matrix products: 12.5 us -> 4.08 us  [body(): jnp.einsum('kij,kjl->kil', lefts, halves, preferred_element_type=jnp.floa...]
    all_to_all x1, waiting for transfers between devices: 15.5 us -> 22.2 us  [body(): lax.all_to_all(outgoing, OPX, split_axis=0, concat_axis=0, tiled=True)]
    all_to_all x1, blocking collectives: 14.4 us -> 10.9 us  [reduce_out(): t = lax.all_to_all(t, 'x', split_axis=0, concat_axis=0, tiled=True)]
    all_to_all x1, blocking collectives: 21.6 us -> 19.5 us  [reduce_out(): t = lax.all_to_all(t, 'zl', split_axis=0, concat_axis=0, tiled=True)]
    gather x0 -> x1, local copies, waits for them, and re-layouts: none -> 2.03 us  [body(): lefts = jnp.take(left_ops[0], left_index[0], axis=0)]
    gather x1, local copies, waits for them, and re-layouts: 0.58 us -> 2.43 us  [body(): outgoing = jnp.take(slabs, wanted, axis=0)]
  transfers between devices with their start and end apart: 1 -> 1, of which waited for: 1 -> 1; matrix products, arithmetic and copies ran while one was open for 1% -> 2% of each run, Pallas kernels for 0% -> 0%
where the time goes in v2:
time: 135 us; the launch traced here: 134 us
  blocking collectives  91.1 us (67%)
  waiting for transfers between devices  22.2 us (16%)
  starting transfers between devices  7.37 us (5%)
  local copies, waits for them, and re-layouts  4.52 us (3%)
  other arithmetic  4.41 us (3%)
  matrix products  4.08 us (3%)
    all_gather x1, blocking collectives, gather_psi(): g = lax.all_gather(g, 'zh', axis=0, tiled=True)  45 us
    all_to_all x1, waiting for transfers between devices, body(): lax.all_to_all(outgoing, OPX, split_axis=0, concat_axis=0, tiled=True)  22.2 us
    all_to_all x1, blocking collectives, reduce_out(): t = lax.all_to_all(t, 'zl', split_axis=0, concat_axis=0, tiled=True)  19.5 us
    all_gather x1, blocking collectives, gather_psi(): g = lax.all_gather(g, 'y', axis=0, tiled=True)  13.7 us
    all_to_all x1, blocking collectives, reduce_out(): t = lax.all_to_all(t, 'x', split_axis=0, concat_axis=0, tiled=True)  10.9 us
    all_to_all x1, starting transfers between devices, body(): lax.all_to_all(outgoing, OPX, split_axis=0, concat_axis=0, tiled=True)  7.37 us
    dot_general x1, matrix products, body(): jnp.einsum('kij,kjl->kil', lefts, halves, preferred_element_type=jnp.floa...  4.08 us
    select_n x2, other arithmetic, body(): outgoing = jnp.take(slabs, wanted, axis=0)  2.78 us
  transfers between devices with their start and end apart: 1, of which 1 were waited for; matrix products, arithmetic and copies ran while one was open for 2% of the time, Pallas kernels for 0%

profile of v2, /device:TPU:8, one launch (start us, length us, event | category | flops | bytes accessed | tf_op | source)
XLA Modules:
  0.0 134.4 jit_solution(8738199644004003101)
XLA Ops:
  0.0 0.0 copy-start
  0.0 0.8 fusion.12
  0.8 0.7 compare_and_fusion
  1.5 2.0 %all_gather.9 = bf16[2,16,512]{2,1,0:T(8,128)(2,1)S(1)} all-gather(bf16[1,16,512]{2,1,0:T(8,128)(2,1)} %param.8), channel_id=1, replica_groups=mesh['y'=4,'zh'=4,'c'=2,'zl'=8,'x'=4] {'c'}, dimensions={0}, use_global_device_ids=true | all-gather | bytes 49152 | tf_op jit(solution)/shard_map/all_gather | solution.py:26
  3.6 45.0 %all_gather.10 = bf16[8,16,512]{2,1,0:T(8,128)(2,1)S(1)} all-gather(bf16[2,16,512]{2,1,0:T(8,128)(2,1)S(1)} %all_gather.9), channel_id=1, replica_groups=mesh['y'=4,'zh'=4,'c'=2,'zl'=8,'x'=4] {'zh'}, dimensions={0}, use_global_device_ids=true | all-gather | bytes 163840 | tf_op jit(solution)/shard_map/all_gather | solution.py:27
  48.5 13.7 %all_gather.11 = bf16[32,16,512]{2,1,0:T(8,128)(2,1)} all-gather(bf16[8,16,512]{2,1,0:T(8,128)(2,1)S(1)} %all_gather.10), channel_id=1, replica_groups=mesh['y'=4,'zh'=4,'c'=2,'zl'=8,'x'=4] {'y'}, dimensions={0}, use_global_device_ids=true | all-gather | bytes 655360 | tf_op jit(solution)/shard_map/all_gather | solution.py:28
  62.3 2.4 %gather_fusion.1 = bf16[32,16,512]{2,1,0:T(8,128)(2,1)} fusion(bf16[32,16,512]{2,1,0:T(8,128)(2,1)} %all_gather.11, s32[1024]{0:T(1024)S(1)} %pad_clamp_fusion), kind=kCustom, calls=%fused_computation.1 | custom fusion | bytes 1048704 | tf_op jit(solution)/shard_map/jit(_take)/gather | solution.py:114
  64.7 2.0 %broadcast_select_fusion = bf16[32,16,512]{2,1,0:T(8,128)(2,1)} fusion(bf16[32,16,512]{2,1,0:T(8,128)(2,1)} %gather_fusion.1, pred[32]{0:T(512)(128)(4,1)S(1)} %compare_and_fusion), kind=kLoop, calls=%fused_computation.11 | loop fusion | flops 262144 | bytes 1048608 | tf_op jit(solution)/shard_map/jit(_take)/select_n | solution.py:114
  66.7 7.4 %all-to-all-start = ((bf16[32,16,512]{2,1,0:T(8,128)(2,1)}), bf16[32,16,512]{2,1,0:T(8,128)(2,1)}, u32[]{:S(2)}, u32[]{:S(2)}) async-start(bf16[32,16,512]{2,1,0:T(8,128)(2,1)} %broadcast_select_fusion), calls=%async_computation | async-start | bytes 1048576 | tf_op jit(solution)/shard_map/all_to_all | solution.py:116
  74.7 0.0 copy-done.4
  74.8 0.0 copy-done.1
  74.8 0.0 copy-start.2
  74.8 0.0 copy-start.3
  74.8 2.0 %gather_fusion = bf16[4,512,512]{2,1,0:T(8,128)(2,1)} fusion(bf16[2,512,512]{2,1,0:T(8,128)(2,1)S(1)} %bitcast.34, s32[1024]{0:T(1024)S(1)} %pad_clamp_fusion.1), kind=kCustom, calls=%fused_computation | custom fusion | bytes 4194320 | tf_op jit(solution)/shard_map/jit(_take)/gather | solution.py:138
  76.8 0.0 copy-done.2
  76.8 0.0 copy-done.3
  76.8 0.2 select_reduce_fusion
  77.0 22.2 %all-to-all-done = bf16[32,16,512]{2,1,0:T(8,128)(2,1)} async-done(((bf16[32,16,512]{2,1,0:T(8,128)(2,1)}), bf16[32,16,512]{2,1,0:T(8,128)(2,1)}, u32[]{:S(2)}, u32[]{:S(2)}) %all-to-all-start) | async-done | bytes 524320 | tf_op jit(solution)/shard_map/all_to_all | solution.py:116
  99.2 0.0 copy-done
  99.2 4.1 %multiply_reduce_fusion = bf16[512,512]{1,0:T(8,128)(2,1)S(1)} fusion(bf16[4,512,512]{2,1,0:T(8,128)(2,1)} %gather_fusion, f32[4]{0:T(128)S(1)} %compare_select_fusion.4, pred[4]{0:T(512)(128)(4,1)S(1)} %compare_and_fusion.1, bf16[512,512,1]{1,0,2:T(8,128)(2,1)} %bitcast.10, bf16[1,4,512,512]{3,2,1,0:T(8,128)(2,1)S(1)} %copy-done), kind=kOutput, calls=%fused_computation.2 | convolution fusion | flops 2151415808 | bytes 5242900 | tf_op jit(solution)/shard_map/kij,kjl->kil/dot_general | solution.py:140
  103.4 10.9 %all_to_all.15 = bf16[4,8,16,512]{3,2,1,0:T(8,128)(2,1)S(1)} all-to-all(bf16[4,8,16,512]{3,2,1,0:T(8,128)(2,1)S(1)} %copy.10), channel_id=1, replica_groups=mesh['y'=4,'zh'=4,'c'=2,'zl'=8,'x'=4] {'x'}, dimensions={0} | all-to-all | bytes 1048576 | tf_op jit(solution)/shard_map/all_to_all | solution.py:85
  114.2 0.1 convert_reduce_fusion
  114.3 19.5 %all_to_all.16 = f32[8,16,512]{2,1,0:T(8,128)S(1)} all-to-all(f32[8,16,512]{2,1,0:T(8,128)S(1)} %convert_reduce_fusion), channel_id=1, replica_groups=mesh['y'=4,'zh'=4,'c'=2,'zl'=8,'x'=4] {'zl'}, dimensions={0} | all-to-all | bytes 524288 | tf_op jit(solution)/shard_map/all_to_all | solution.py:87
  133.8 0.6 reduce_sum.39
  (8 shorter events, 0.1 us)
Async XLA Ops:
  0.0 99.2 %copy-start = (bf16[1,4,512,512]{3,2,1,0:T(8,128)(2,1)S(1)}, bf16[1,4,512,512]{3,2,1,0:T(8,128)(2,1)}, u32[]{:S(2)}) copy-start(bf16[1,4,512,512]{3,2,1,0:T(8,128)(2,1)} %param.15) | copy-start | bytes 6291460
  0.0 74.7 %copy-start.4 = (s32[1,4]{1,0:T(1,128)S(1)}, s32[1,4]{1,0:T(1,128)}, u32[]{:S(2)}) copy-start(s32[1,4]{1,0:T(1,128)} %param.12) | copy-start | bytes 52
  0.0 74.7 %copy-start.1 = (bf16[1,2,512,512]{3,2,1,0:T(8,128)(2,1)S(1)}, bf16[1,2,512,512]{3,2,1,0:T(8,128)(2,1)}, u32[]{:S(2)}) copy-start(bf16[1,2,512,512]{3,2,1,0:T(8,128)(2,1)} %param.14) | copy-start | bytes 3145732
  66.7 32.5 %all-to-all-start = ((bf16[32,16,512]{2,1,0:T(8,128)(2,1)}), bf16[32,16,512]{2,1,0:T(8,128)(2,1)}, u32[]{:S(2)}, u32[]{:S(2)}) async-start(bf16[32,16,512]{2,1,0:T(8,128)(2,1)} %broadcast_select_fusion), calls=%async_computation | async-start | bytes 1048576 | tf_op jit(solution)/shard_map/all_to_all | solution.py:116
  74.8 2.1 %copy-start.2 = (f32[64]{0:T(128)S(1)}, f32[64]{0:T(128)}, u32[]{:S(2)}) copy-start(f32[64]{0:T(128)} %param.13) | copy-start | bytes 772
  74.8 2.0 %copy-start.3 = (s32[1,4]{1,0:T(1,128)S(1)}, s32[1,4]{1,0:T(1,128)}, u32[]{:S(2)}) copy-start(s32[1,4]{1,0:T(1,128)} %param.11) | copy-start | bytes 52

commit v3 on v2

--- a/solution.py
+++ b/solution.py
@@ -8,6 +8,7 @@
 REDUCE = "h_a2a_xbf"
 ROUTE = "flat"
 COMPUTE = "batch"
+TAKE = "clip"
 
 SEC = ("y", "zh", "c")
 OPX = ("zl", "x")
@@ -37,6 +38,15 @@
         g = lax.all_gather(g, "zh", axis=0, tiled=True)
         g = lax.all_gather(g, "c", axis=0, tiled=True)
         return g, lambda s: (s % 2) * 16 + ((s % 8) // 2) * 4 + s // 8
+    if GATHER == "c_zpp_y":
+        g = lax.all_gather(psi, "c", axis=0, tiled=True)
+        zi = lax.axis_index("zh")
+        recv = [g] + [lax.ppermute(g, "zh", [(i, (i + d) % 4) for i in range(4)]) for d in range(1, 4)]
+        st = jnp.stack(recv)
+        order = (zi - jnp.arange(4)) % 4
+        g = jnp.take(st, order, axis=0, mode="clip").reshape((8,) + g.shape[1:])
+        g = lax.all_gather(g, "y", axis=0, tiled=True)
+        return g, lambda s: s
     if GATHER == "c_yz":
         g = lax.all_gather(psi, "c", axis=0, tiled=True)
         g = lax.all_gather(g, ("y", "zh"), axis=0, tiled=True)
@@ -111,7 +121,7 @@
     width = psi.shape[2]
     slabs, remap = gather_psi(psi)
     wanted = remap(in_sector[0])
-    outgoing = jnp.take(slabs, wanted, axis=0)
+    outgoing = jnp.take(slabs, wanted, axis=0, mode=TAKE)
     if ROUTE == "flat":
         arrived = lax.all_to_all(outgoing, OPX, split_axis=0, concat_axis=0, tiled=True)
     else:

time: 135 us -> 132 us (0.978)
  other arithmetic: 4.41 us -> 1.72 us
    select_n x2 -> x0, other arithmetic: 2.78 us -> none  [body(): outgoing = jnp.take(slabs, wanted, axis=0)]
where the time goes in v3:
time: 132 us
  blocking collectives  91.2 us (69%)
  waiting for transfers between devices  22.2 us (17%)
  starting transfers between devices  7.37 us (6%)
  local copies, waits for them, and re-layouts  4.51 us (3%)
  matrix products  4.08 us (3%)
  other arithmetic  1.72 us (1%)
    all_gather x1, blocking collectives, gather_psi(): g = lax.all_gather(g, 'zh', axis=0, tiled=True)  45 us
    all_to_all x1, waiting for transfers between devices, body(): lax.all_to_all(outgoing, OPX, split_axis=0, concat_axis=0, tiled=True)  22.2 us
    all_to_all x1, blocking collectives, reduce_out(): t = lax.all_to_all(t, 'zl', split_axis=0, concat_axis=0, tiled=True)  19.5 us
    all_gather x1, blocking collectives, gather_psi(): g = lax.all_gather(g, 'y', axis=0, tiled=True)  13.7 us
    all_to_all x1, blocking collectives, reduce_out(): t = lax.all_to_all(t, 'x', split_axis=0, concat_axis=0, tiled=True)  10.9 us
    all_to_all x1, starting transfers between devices, body(): lax.all_to_all(outgoing, OPX, split_axis=0, concat_axis=0, tiled=True)  7.37 us
    dot_general x1, matrix products, body(): jnp.einsum('kij,kjl->kil', lefts, halves, preferred_element_type=jnp.floa...  4.08 us
  transfers between devices with their start and end apart: 1, of which 1 were waited for; matrix products, arithmetic and copies ran while one was open for 2% of the time, Pallas kernels for 0%

profile of v3, /device:TPU:8, one launch (start us, length us, event | category | flops | bytes accessed | tf_op | source)
XLA Modules:
  0.0 131.8 jit_solution(8861990208014332529)
XLA Ops:
  0.0 0.0 copy-start
  0.0 0.0 copy-start.4
  0.0 0.0 copy-start.1
  0.0 0.8 pad_clamp_fusion
  0.8 2.2 %all_gather.9 = bf16[2,16,512]{2,1,0:T(8,128)(2,1)S(1)} all-gather(bf16[1,16,512]{2,1,0:T(8,128)(2,1)} %param.8), channel_id=1, replica_groups=mesh['y'=4,'zh'=4,'c'=2,'zl'=8,'x'=4] {'c'}, dimensions={0}, use_global_device_ids=true | all-gather | bytes 49152 | tf_op jit(solution)/shard_map/all_gather | solution.py:27
  3.0 45.0 %all_gather.10 = bf16[8,16,512]{2,1,0:T(8,128)(2,1)S(1)} all-gather(bf16[2,16,512]{2,1,0:T(8,128)(2,1)S(1)} %all_gather.9), channel_id=1, replica_groups=mesh['y'=4,'zh'=4,'c'=2,'zl'=8,'x'=4] {'zh'}, dimensions={0}, use_global_device_ids=true | all-gather | bytes 163840 | tf_op jit(solution)/shard_map/all_gather | solution.py:28
  47.9 13.7 %all_gather.11 = bf16[32,16,512]{2,1,0:T(8,128)(2,1)} all-gather(bf16[8,16,512]{2,1,0:T(8,128)(2,1)S(1)} %all_gather.10), channel_id=1, replica_groups=mesh['y'=4,'zh'=4,'c'=2,'zl'=8,'x'=4] {'y'}, dimensions={0}, use_global_device_ids=true | all-gather | bytes 655360 | tf_op jit(solution)/shard_map/all_gather | solution.py:29
  61.7 2.4 %gather_fusion.1 = bf16[32,16,512]{2,1,0:T(8,128)(2,1)} fusion(bf16[32,16,512]{2,1,0:T(8,128)(2,1)} %all_gather.11, s32[1024]{0:T(1024)S(1)} %pad_clamp_fusion), kind=kCustom, calls=%fused_computation.1 | custom fusion | bytes 1048704 | tf_op jit(solution)/shard_map/jit(_take)/gather | solution.py:124
  64.1 7.4 %all-to-all-start = ((bf16[32,16,512]{2,1,0:T(8,128)(2,1)}), bf16[32,16,512]{2,1,0:T(8,128)(2,1)}, u32[]{:S(2)}, u32[]{:S(2)}) async-start(bf16[32,16,512]{2,1,0:T(8,128)(2,1)} %gather_fusion.1), calls=%async_computation | async-start | bytes 1048576 | tf_op jit(solution)/shard_map/all_to_all | solution.py:126
  72.1 0.0 copy-done.4
  72.2 0.0 copy-done.1
  72.2 0.0 copy-start.2
  72.2 0.0 copy-start.3
  72.2 2.0 %gather_fusion = bf16[4,512,512]{2,1,0:T(8,128)(2,1)} fusion(bf16[2,512,512]{2,1,0:T(8,128)(2,1)S(1)} %bitcast.29, s32[1024]{0:T(1024)S(1)} %pad_clamp_fusion.1), kind=kCustom, calls=%fused_computation | custom fusion | bytes 4194320 | tf_op jit(solution)/shard_map/jit(_take)/gather | solution.py:148
  74.2 0.0 copy-done.2
  74.2 0.0 copy-done.3
  74.2 0.2 select_reduce_fusion
  74.4 22.2 %all-to-all-done = bf16[32,16,512]{2,1,0:T(8,128)(2,1)} async-done(((bf16[32,16,512]{2,1,0:T(8,128)(2,1)}), bf16[32,16,512]{2,1,0:T(8,128)(2,1)}, u32[]{:S(2)}, u32[]{:S(2)}) %all-to-all-start) | async-done | bytes 524320 | tf_op jit(solution)/shard_map/all_to_all | solution.py:126
  96.6 0.0 copy-done
  96.6 4.1 %multiply_reduce_fusion = bf16[512,512]{1,0:T(8,128)(2,1)S(1)} fusion(bf16[4,512,512]{2,1,0:T(8,128)(2,1)} %gather_fusion, f32[4]{0:T(128)S(1)} %compare_select_fusion.2, pred[4]{0:T(512)(128)(4,1)S(1)} %compare_and_fusion, bf16[512,512,1]{1,0,2:T(8,128)(2,1)} %bitcast.8, bf16[1,4,512,512]{3,2,1,0:T(8,128)(2,1)S(1)} %copy-done), kind=kOutput, calls=%fused_computation.2 | convolution fusion | flops 2151415808 | bytes 5242900 | tf_op jit(solution)/shard_map/kij,kjl->kil/dot_general | solution.py:150
  100.8 10.9 %all_to_all.15 = bf16[4,8,16,512]{3,2,1,0:T(8,128)(2,1)S(1)} all-to-all(bf16[4,8,16,512]{3,2,1,0:T(8,128)(2,1)S(1)} %copy.10), channel_id=1, replica_groups=mesh['y'=4,'zh'=4,'c'=2,'zl'=8,'x'=4] {'x'}, dimensions={0} | all-to-all | bytes 1048576 | tf_op jit(solution)/shard_map/all_to_all | solution.py:95
  111.7 0.1 convert_reduce_fusion
  111.7 19.5 %all_to_all.16 = f32[8,16,512]{2,1,0:T(8,128)S(1)} all-to-all(f32[8,16,512]{2,1,0:T(8,128)S(1)} %convert_reduce_fusion), channel_id=1, replica_groups=mesh['y'=4,'zh'=4,'c'=2,'zl'=8,'x'=4] {'zl'}, dimensions={0} | all-to-all | bytes 524288 | tf_op jit(solution)/shard_map/all_to_all | solution.py:97
  131.2 0.6 reduce_sum.39
  (5 shorter events, 0.1 us)
Async XLA Ops:
  0.0 96.6 %copy-start = (bf16[1,4,512,512]{3,2,1,0:T(8,128)(2,1)S(1)}, bf16[1,4,512,512]{3,2,1,0:T(8,128)(2,1)}, u32[]{:S(2)}) copy-start(bf16[1,4,512,512]{3,2,1,0:T(8,128)(2,1)} %param.15) | copy-start | bytes 6291460
  0.0 72.1 %copy-start.4 = (s32[1,4]{1,0:T(1,128)S(1)}, s32[1,4]{1,0:T(1,128)}, u32[]{:S(2)}) copy-start(s32[1,4]{1,0:T(1,128)} %param.12) | copy-start | bytes 52
  0.0 72.2 %copy-start.1 = (bf16[1,2,512,512]{3,2,1,0:T(8,128)(2,1)S(1)}, bf16[1,2,512,512]{3,2,1,0:T(8,128)(2,1)}, u32[]{:S(2)}) copy-start(bf16[1,2,512,512]{3,2,1,0:T(8,128)(2,1)} %param.14) | copy-start | bytes 3145732
  64.1 32.5 %all-to-all-start = ((bf16[32,16,512]{2,1,0:T(8,128)(2,1)}), bf16[32,16,512]{2,1,0:T(8,128)(2,1)}, u32[]{:S(2)}, u32[]{:S(2)}) async-start(bf16[32,16,512]{2,1,0:T(8,128)(2,1)} %gather_fusion.1), calls=%async_computation | async-start | bytes 1048576 | tf_op jit(solution)/shard_map/all_to_all | solution.py:126
  72.2 2.1 %copy-start.2 = (f32[64]{0:T(128)S(1)}, f32[64]{0:T(128)}, u32[]{:S(2)}) copy-start(f32[64]{0:T(128)} %param.13) | copy-start | bytes 772
  72.2 2.0 %copy-start.3 = (s32[1,4]{1,0:T(1,128)S(1)}, s32[1,4]{1,0:T(1,128)}, u32[]{:S(2)}) copy-start(s32[1,4]{1,0:T(1,128)} %param.11) | copy-start | bytes 52

commit v4 on v3

--- a/solution.py
+++ b/solution.py
@@ -8,7 +8,7 @@
 REDUCE = "h_a2a_xbf"
 ROUTE = "flat"
 COMPUTE = "batch"
-TAKE = "clip"
+TAKE = "onehot"
 
 SEC = ("y", "zh", "c")
 OPX = ("zl", "x")
@@ -121,7 +121,12 @@
     width = psi.shape[2]
     slabs, remap = gather_psi(psi)
     wanted = remap(in_sector[0])
-    outgoing = jnp.take(slabs, wanted, axis=0, mode=TAKE)
+    if TAKE == "onehot":
+        pick = (wanted[:, None] == jnp.arange(slabs.shape[0], dtype=jnp.int32)[None, :]).astype(slabs.dtype)
+        flat = slabs.reshape(slabs.shape[0], slab_rows * width)
+        outgoing = jnp.dot(pick, flat, preferred_element_type=jnp.float32).astype(slabs.dtype).reshape(slabs.shape)
+    else:
+        outgoing = jnp.take(slabs, wanted, axis=0, mode=TAKE)
     if ROUTE == "flat":
         arrived = lax.all_to_all(outgoing, OPX, split_axis=0, concat_axis=0, tiled=True)
     else:

time: 132 us -> 130 us (0.985)
    gather x1 -> x0, local copies, waits for them, and re-layouts: 2.42 us -> none  [body(): outgoing = jnp.take(slabs, wanted, axis=0, mode=TAKE)]
where the time goes in v4:
time: 130 us
  blocking collectives  90.5 us (70%)
  waiting for transfers between devices  22.3 us (17%)
  starting transfers between devices  7.1 us (5%)
  matrix products  5.12 us (4%)
  local copies, waits for them, and re-layouts  3.36 us (3%)
    all_gather x1, blocking collectives, gather_psi(): g = lax.all_gather(g, 'zh', axis=0, tiled=True)  45 us
    all_to_all x1, waiting for transfers between devices, body(): lax.all_to_all(outgoing, OPX, split_axis=0, concat_axis=0, tiled=True)  22.3 us
    all_to_all x1, blocking collectives, reduce_out(): t = lax.all_to_all(t, 'zl', split_axis=0, concat_axis=0, tiled=True)  19.5 us
    all_gather x1, blocking collectives, gather_psi(): g = lax.all_gather(g, 'y', axis=0, tiled=True)  13 us
    all_to_all x1, blocking collectives, reduce_out(): t = lax.all_to_all(t, 'x', split_axis=0, concat_axis=0, tiled=True)  10.9 us
    all_to_all x1, starting transfers between devices, body(): lax.all_to_all(outgoing, OPX, split_axis=0, concat_axis=0, tiled=True)  7.1 us
    dot_general x1, matrix products, body(): jnp.einsum('kij,kjl->kil', lefts, halves, preferred_element_type=jnp.floa...  4.08 us
  transfers between devices with their start and end apart: 1, of which 1 were waited for; matrix products, arithmetic and copies ran while one was open for 2% of the time, Pallas kernels for 0%

profile of v4, /device:TPU:8, one launch (start us, length us, event | category | flops | bytes accessed | tf_op | source)
XLA Modules:
  0.0 130.1 jit_solution(13936743018248795585)
XLA Ops:
  0.0 0.0 copy-start
  0.0 2.2 %all_gather.9 = bf16[2,16,512]{2,1,0:T(8,128)(2,1)S(1)} all-gather(bf16[1,16,512]{2,1,0:T(8,128)(2,1)} %param.8), channel_id=1, replica_groups=mesh['y'=4,'zh'=4,'c'=2,'zl'=8,'x'=4] {'c'}, dimensions={0}, use_global_device_ids=true | all-gather | bytes 49152 | tf_op jit(solution)/shard_map/all_gather | solution.py:27
  2.2 45.0 %all_gather.10 = bf16[8,16,512]{2,1,0:T(8,128)(2,1)S(1)} all-gather(bf16[2,16,512]{2,1,0:T(8,128)(2,1)S(1)} %all_gather.9), channel_id=1, replica_groups=mesh['y'=4,'zh'=4,'c'=2,'zl'=8,'x'=4] {'zh'}, dimensions={0}, use_global_device_ids=true | all-gather | bytes 163840 | tf_op jit(solution)/shard_map/all_gather | solution.py:28
  47.1 13.0 %all_gather.11 = bf16[32,16,512]{2,1,0:T(8,128)(2,1)S(1)} all-gather(bf16[8,16,512]{2,1,0:T(8,128)(2,1)S(1)} %all_gather.10), channel_id=1, replica_groups=mesh['y'=4,'zh'=4,'c'=2,'zl'=8,'x'=4] {'y'}, dimensions={0}, use_global_device_ids=true | all-gather | bytes 655360 | tf_op jit(solution)/shard_map/all_gather | solution.py:29
  60.1 0.0 copy-start.4
  60.1 0.3 copy.11
  60.4 1.0 convolution_convert_fusion
  61.5 1.0 copy.12
  62.4 7.1 %all-to-all-start = ((bf16[32,16,512]{2,1,0:T(8,128)(2,1)}), bf16[32,16,512]{2,1,0:T(8,128)(2,1)}, u32[]{:S(2)}, u32[]{:S(2)}) async-start(bf16[32,16,512]{2,1,0:T(8,128)(2,1)} %bitcast.36), calls=%async_computation | async-start | bytes 1048576 | tf_op jit(solution)/shard_map/all_to_all | solution.py:131
  70.2 0.0 copy-done.4
  70.2 0.0 copy-done.1
  70.2 0.0 copy-start.2
  70.3 0.0 copy-start.3
  70.3 2.0 %gather_fusion = bf16[4,512,512]{2,1,0:T(8,128)(2,1)} fusion(bf16[2,512,512]{2,1,0:T(8,128)(2,1)S(1)} %bitcast.34, s32[1024]{0:T(1024)S(1)} %pad_clamp_fusion), kind=kCustom, calls=%fused_computation | custom fusion | bytes 4194320 | tf_op jit(solution)/shard_map/jit(_take)/gather | solution.py:153
  72.3 0.0 copy-done.2
  72.3 0.0 copy-done.3
  72.3 0.2 select_reduce_fusion
  72.5 22.3 %all-to-all-done = bf16[32,16,512]{2,1,0:T(8,128)(2,1)} async-done(((bf16[32,16,512]{2,1,0:T(8,128)(2,1)}), bf16[32,16,512]{2,1,0:T(8,128)(2,1)}, u32[]{:S(2)}, u32[]{:S(2)}) %all-to-all-start) | async-done | bytes 524320 | tf_op jit(solution)/shard_map/all_to_all | solution.py:131
  94.8 0.0 copy-done
  94.8 4.1 %multiply_reduce_fusion = bf16[512,512]{1,0:T(8,128)(2,1)S(1)} fusion(bf16[4,512,512]{2,1,0:T(8,128)(2,1)} %gather_fusion, f32[4]{0:T(128)S(1)} %compare_select_fusion.2, pred[4]{0:T(512)(128)(4,1)S(1)} %compare_and_fusion, bf16[512,512,1]{1,0,2:T(8,128)(2,1)} %bitcast.8, bf16[1,4,512,512]{3,2,1,0:T(8,128)(2,1)S(1)} %copy-done), kind=kOutput, calls=%fused_computation.2 | convolution fusion | flops 2151415808 | bytes 5242900 | tf_op jit(solution)/shard_map/kij,kjl->kil/dot_general | solution.py:155
  99.0 10.9 %all_to_all.15 = bf16[4,8,16,512]{3,2,1,0:T(8,128)(2,1)S(1)} all-to-all(bf16[4,8,16,512]{3,2,1,0:T(8,128)(2,1)S(1)} %copy.10), channel_id=1, replica_groups=mesh['y'=4,'zh'=4,'c'=2,'zl'=8,'x'=4] {'x'}, dimensions={0} | all-to-all | bytes 1048576 | tf_op jit(solution)/shard_map/all_to_all | solution.py:95
  109.8 0.1 convert_reduce_fusion
  109.9 19.5 %all_to_all.16 = f32[8,16,512]{2,1,0:T(8,128)S(1)} all-to-all(f32[8,16,512]{2,1,0:T(8,128)S(1)} %convert_reduce_fusion), channel_id=1, replica_groups=mesh['y'=4,'zh'=4,'c'=2,'zl'=8,'x'=4] {'zl'}, dimensions={0} | all-to-all | bytes 524288 | tf_op jit(solution)/shard_map/all_to_all | solution.py:97
  129.4 0.6 reduce_sum.39
  (6 shorter events, 0.1 us)
Async XLA Ops:
  0.0 94.8 %copy-start = (bf16[1,4,512,512]{3,2,1,0:T(8,128)(2,1)S(1)}, bf16[1,4,512,512]{3,2,1,0:T(8,128)(2,1)}, u32[]{:S(2)}) copy-start(bf16[1,4,512,512]{3,2,1,0:T(8,128)(2,1)} %param.15) | copy-start | bytes 6291460
  60.1 10.1 %copy-start.4 = (s32[1,4]{1,0:T(1,128)S(1)}, s32[1,4]{1,0:T(1,128)}, u32[]{:S(2)}) copy-start(s32[1,4]{1,0:T(1,128)} %param.12) | copy-start | bytes 52
  60.1 10.1 %copy-start.1 = (bf16[1,2,512,512]{3,2,1,0:T(8,128)(2,1)S(1)}, bf16[1,2,512,512]{3,2,1,0:T(8,128)(2,1)}, u32[]{:S(2)}) copy-start(bf16[1,2,512,512]{3,2,1,0:T(8,128)(2,1)} %param.14) | copy-start | bytes 3145732
  62.4 32.4 %all-to-all-start = ((bf16[32,16,512]{2,1,0:T(8,128)(2,1)}), bf16[32,16,512]{2,1,0:T(8,128)(2,1)}, u32[]{:S(2)}, u32[]{:S(2)}) async-start(bf16[32,16,512]{2,1,0:T(8,128)(2,1)} %bitcast.36), calls=%async_computation | async-start | bytes 1048576 | tf_op jit(solution)/shard_map/all_to_all | solution.py:131
  70.2 2.1 %copy-start.2 = (f32[64]{0:T(128)S(1)}, f32[64]{0:T(128)}, u32[]{:S(2)}) copy-start(f32[64]{0:T(128)} %param.13) | copy-start | bytes 772
  70.3 2.0 %copy-start.3 = (s32[1,4]{1,0:T(1,128)S(1)}, s32[1,4]{1,0:T(1,128)}, u32[]{:S(2)}) copy-start(s32[1,4]{1,0:T(1,128)} %param.11) | copy-start | bytes 52

commit v5 on v4

--- a/solution.py
+++ b/solution.py
@@ -5,7 +5,7 @@
 from jax.sharding import Mesh, PartitionSpec as P
 
 GATHER = "h_czy"
-REDUCE = "h_a2a_xbf"
+REDUCE = "h_a2a"
 ROUTE = "flat"
 COMPUTE = "batch"
 TAKE = "onehot"

time: 130 us -> 136 us (1.046)
  blocking collectives: 90.5 us -> 96.1 us
    all_to_all x1, blocking collectives: 10.9 us -> 14.4 us  [reduce_out(): t = lax.all_to_all(t, 'x', split_axis=0, concat_axis=0, tiled=True)]
    all_to_all x1, blocking collectives: 19.5 us -> 21.6 us  [reduce_out(): t = lax.all_to_all(t, 'zl', split_axis=0, concat_axis=0, tiled=True)]
where the time goes in v5:
time: 136 us
  blocking collectives  96.1 us (71%)
  waiting for transfers between devices  22.3 us (16%)
  starting transfers between devices  7.1 us (5%)
  matrix products  5.15 us (4%)
  local copies, waits for them, and re-layouts  3.4 us (2%)
    all_gather x1, blocking collectives, gather_psi(): g = lax.all_gather(g, 'zh', axis=0, tiled=True)  45 us
    all_to_all x1, waiting for transfers between devices, body(): lax.all_to_all(outgoing, OPX, split_axis=0, concat_axis=0, tiled=True)  22.3 us
    all_to_all x1, blocking collectives, reduce_out(): t = lax.all_to_all(t, 'zl', split_axis=0, concat_axis=0, tiled=True)  21.6 us
    all_to_all x1, blocking collectives, reduce_out(): t = lax.all_to_all(t, 'x', split_axis=0, concat_axis=0, tiled=True)  14.4 us
    all_gather x1, blocking collectives, gather_psi(): g = lax.all_gather(g, 'y', axis=0, tiled=True)  13 us
    all_to_all x1, starting transfers between devices, body(): lax.all_to_all(outgoing, OPX, split_axis=0, concat_axis=0, tiled=True)  7.1 us
    dot_general x1, matrix products, body(): jnp.einsum('kij,kjl->kil', lefts, halves, preferred_element_type=jnp.floa...  4.11 us
  transfers between devices with their start and end apart: 1, of which 1 were waited for; matrix products, arithmetic and copies ran while one was open for 2% of the time, Pallas kernels for 0%

profile of v5, /device:TPU:8, one launch (start us, length us, event | category | flops | bytes accessed | tf_op | source)
XLA Modules:
  0.0 135.8 jit_solution(16517463774201062713)
XLA Ops:
  0.0 0.0 copy-start
  0.0 2.2 %all_gather.9 = bf16[2,16,512]{2,1,0:T(8,128)(2,1)S(1)} all-gather(bf16[1,16,512]{2,1,0:T(8,128)(2,1)} %param.8), channel_id=1, replica_groups=mesh['y'=4,'zh'=4,'c'=2,'zl'=8,'x'=4] {'c'}, dimensions={0}, use_global_device_ids=true | all-gather | bytes 49152 | tf_op jit(solution)/shard_map/all_gather | solution.py:27
  2.2 45.0 %all_gather.10 = bf16[8,16,512]{2,1,0:T(8,128)(2,1)S(1)} all-gather(bf16[2,16,512]{2,1,0:T(8,128)(2,1)S(1)} %all_gather.9), channel_id=1, replica_groups=mesh['y'=4,'zh'=4,'c'=2,'zl'=8,'x'=4] {'zh'}, dimensions={0}, use_global_device_ids=true | all-gather | bytes 163840 | tf_op jit(solution)/shard_map/all_gather | solution.py:28
  47.1 13.0 %all_gather.11 = bf16[32,16,512]{2,1,0:T(8,128)(2,1)S(1)} all-gather(bf16[8,16,512]{2,1,0:T(8,128)(2,1)S(1)} %all_gather.10), channel_id=1, replica_groups=mesh['y'=4,'zh'=4,'c'=2,'zl'=8,'x'=4] {'y'}, dimensions={0}, use_global_device_ids=true | all-gather | bytes 655360 | tf_op jit(solution)/shard_map/all_gather | solution.py:29
  60.1 0.3 copy.11
  60.4 1.0 convolution_convert_fusion
  61.5 1.0 copy.12
  62.4 7.1 %all-to-all-start = ((bf16[32,16,512]{2,1,0:T(8,128)(2,1)}), bf16[32,16,512]{2,1,0:T(8,128)(2,1)}, u32[]{:S(2)}, u32[]{:S(2)}) async-start(bf16[32,16,512]{2,1,0:T(8,128)(2,1)} %bitcast.36), calls=%async_computation | async-start | bytes 1048576 | tf_op jit(solution)/shard_map/all_to_all | solution.py:131
  70.2 0.0 copy-done.4
  70.2 0.0 copy-done.1
  70.2 0.0 copy-start.2
  70.3 0.0 copy-start.3
  70.3 2.0 %gather_fusion = bf16[4,512,512]{2,1,0:T(8,128)(2,1)} fusion(bf16[2,512,512]{2,1,0:T(8,128)(2,1)S(1)} %bitcast.34, s32[1024]{0:T(1024)S(1)} %pad_clamp_fusion), kind=kCustom, calls=%fused_computation | custom fusion | bytes 4194320 | tf_op jit(solution)/shard_map/jit(_take)/gather | solution.py:153
  72.3 0.0 copy-done.2
  72.3 0.0 copy-done.3
  72.3 0.2 select_reduce_fusion
  72.5 22.3 %all-to-all-done = bf16[32,16,512]{2,1,0:T(8,128)(2,1)} async-done(((bf16[32,16,512]{2,1,0:T(8,128)(2,1)}), bf16[32,16,512]{2,1,0:T(8,128)(2,1)}, u32[]{:S(2)}, u32[]{:S(2)}) %all-to-all-start) | async-done | bytes 524320 | tf_op jit(solution)/shard_map/all_to_all | solution.py:131
  94.8 0.0 copy-done
  94.8 4.1 %multiply_reduce_fusion = f32[512,512]{1,0:T(8,128)S(1)} fusion(bf16[4,512,512]{2,1,0:T(8,128)(2,1)} %gather_fusion, f32[4]{0:T(128)S(1)} %compare_select_fusion.2, pred[4]{0:T(512)(128)(4,1)S(1)} %compare_and_fusion, bf16[512,512,1]{1,0,2:T(8,128)(2,1)} %bitcast.8, bf16[1,4,512,512]{3,2,1,0:T(8,128)(2,1)S(1)} %copy-done), kind=kOutput, calls=%fused_computation.2 | convolution fusion | flops 2151415808 | bytes 5767188 | tf_op jit(solution)/shard_map/kij,kjl->kil/dot_general | solution.py:155
  98.9 0.1 copy.10
  99.0 14.4 %all_to_all.15 = f32[4,8,16,512]{3,2,1,0:T(8,128)S(1)} all-to-all(f32[4,8,16,512]{3,2,1,0:T(8,128)S(1)} %copy.10), channel_id=1, replica_groups=mesh['y'=4,'zh'=4,'c'=2,'zl'=8,'x'=4] {'x'}, dimensions={0} | all-to-all | bytes 2097152 | tf_op jit(solution)/shard_map/all_to_all | solution.py:101
  113.4 0.1 reduce_sum.38
  113.5 21.6 %all_to_all.16 = f32[8,16,512]{2,1,0:T(8,128)S(1)} all-to-all(f32[8,16,512]{2,1,0:T(8,128)S(1)} %reduce_sum.38), channel_id=1, replica_groups=mesh['y'=4,'zh'=4,'c'=2,'zl'=8,'x'=4] {'zl'}, dimensions={0} | all-to-all | bytes 524288 | tf_op jit(solution)/shard_map/all_to_all | solution.py:103
  135.1 0.6 reduce_sum.39
  (6 shorter events, 0.0 us)
Async XLA Ops:
  0.0 94.8 %copy-start = (bf16[1,4,512,512]{3,2,1,0:T(8,128)(2,1)S(1)}, bf16[1,4,512,512]{3,2,1,0:T(8,128)(2,1)}, u32[]{:S(2)}) copy-start(bf16[1,4,512,512]{3,2,1,0:T(8,128)(2,1)} %param.15) | copy-start | bytes 6291460
  60.1 10.1 %copy-start.4 = (s32[1,4]{1,0:T(1,128)S(1)}, s32[1,4]{1,0:T(1,128)}, u32[]{:S(2)}) copy-start(s32[1,4]{1,0:T(1,128)} %param.12) | copy-start | bytes 52
  60.1 10.1 %copy-start.1 = (bf16[1,2,512,512]{3,2,1,0:T(8,128)(2,1)S(1)}, bf16[1,2,512,512]{3,2,1,0:T(8,128)(2,1)}, u32[]{:S(2)}) copy-start(bf16[1,2,512,512]{3,2,1,0:T(8,128)(2,1)} %param.14) | copy-start | bytes 3145732
  62.4 32.4 %all-to-all-start = ((bf16[32,16,512]{2,1,0:T(8,128)(2,1)}), bf16[32,16,512]{2,1,0:T(8,128)(2,1)}, u32[]{:S(2)}, u32[]{:S(2)}) async-start(bf16[32,16,512]{2,1,0:T(8,128)(2,1)} %bitcast.36), calls=%async_computation | async-start | bytes 1048576 | tf_op jit(solution)/shard_map/all_to_all | solution.py:131
  70.2 2.1 %copy-start.2 = (f32[64]{0:T(128)S(1)}, f32[64]{0:T(128)}, u32[]{:S(2)}) copy-start(f32[64]{0:T(128)} %param.13) | copy-start | bytes 772
  70.3 2.0 %copy-start.3 = (s32[1,4]{1,0:T(1,128)S(1)}, s32[1,4]{1,0:T(1,128)}, u32[]{:S(2)}) copy-start(s32[1,4]{1,0:T(1,128)} %param.11) | copy-start | bytes 52

commit v6 on v4

--- a/solution.py
+++ b/solution.py
@@ -123,8 +123,7 @@
     wanted = remap(in_sector[0])
     if TAKE == "onehot":
         pick = (wanted[:, None] == jnp.arange(slabs.shape[0], dtype=jnp.int32)[None, :]).astype(slabs.dtype)
-        flat = slabs.reshape(slabs.shape[0], slab_rows * width)
-        outgoing = jnp.dot(pick, flat, preferred_element_type=jnp.float32).astype(slabs.dtype).reshape(slabs.shape)
+        outgoing = jnp.einsum("od,dij->oij", pick, slabs, preferred_element_type=jnp.float32).astype(slabs.dtype)
     else:
         outgoing = jnp.take(slabs, wanted, axis=0, mode=TAKE)
     if ROUTE == "flat":

time: 130 us -> 130 us (level)
  no operation moved by 1% of the time
where the time goes in v6:
time: 130 us; the launch traced here: 129 us
  blocking collectives  89.9 us (69%)
  waiting for transfers between devices  21.6 us (17%)
  starting transfers between devices  7.74 us (6%)
  matrix products  5.08 us (4%)
  local copies, waits for them, and re-layouts  3.27 us (3%)
    all_gather x1, blocking collectives, gather_psi(): g = lax.all_gather(g, 'zh', axis=0, tiled=True)  45.1 us
    all_to_all x1, waiting for transfers between devices, body(): lax.all_to_all(outgoing, OPX, split_axis=0, concat_axis=0, tiled=True)  21.6 us
    all_to_all x1, blocking collectives, reduce_out(): t = lax.all_to_all(t, 'zl', split_axis=0, concat_axis=0, tiled=True)  18.8 us
    all_gather x1, blocking collectives, gather_psi(): g = lax.all_gather(g, 'y', axis=0, tiled=True)  13 us
    all_to_all x1, blocking collectives, reduce_out(): t = lax.all_to_all(t, 'x', split_axis=0, concat_axis=0, tiled=True)  10.9 us
    all_to_all x1, starting transfers between devices, body(): lax.all_to_all(outgoing, OPX, split_axis=0, concat_axis=0, tiled=True)  7.74 us
    dot_general x1, matrix products, body(): jnp.einsum('kij,kjl->kil', lefts, halves, preferred_element_type=jnp.floa...  4.08 us
  transfers between devices with their start and end apart: 1, of which 1 were waited for; matrix products, arithmetic and copies ran while one was open for 2% of the time, Pallas kernels for 0%

profile of v6, /device:TPU:8, one launch (start us, length us, event | category | flops | bytes accessed | tf_op | source)
XLA Modules:
  0.0 129.3 jit_solution(9334734489497767215)
XLA Ops:
  0.0 0.0 copy-start
  0.0 2.2 %all_gather.9 = bf16[2,16,512]{2,1,0:T(8,128)(2,1)S(1)} all-gather(bf16[1,16,512]{2,1,0:T(8,128)(2,1)} %param.8), channel_id=1, replica_groups=mesh['y'=4,'zh'=4,'c'=2,'zl'=8,'x'=4] {'c'}, dimensions={0}, use_global_device_ids=true | all-gather | bytes 49152 | tf_op jit(solution)/shard_map/all_gather | solution.py:27
  2.2 0.0 copy-start.4
  2.2 45.1 %all_gather.10 = bf16[8,16,512]{2,1,0:T(8,128)(2,1)S(1)} all-gather(bf16[2,16,512]{2,1,0:T(8,128)(2,1)S(1)} %all_gather.9), channel_id=1, replica_groups=mesh['y'=4,'zh'=4,'c'=2,'zl'=8,'x'=4] {'zh'}, dimensions={0}, use_global_device_ids=true | all-gather | bytes 163840 | tf_op jit(solution)/shard_map/all_gather | solution.py:28
  47.3 0.1 copy.17
  47.4 13.0 %all_gather.11 = bf16[32,16,512]{2,0,1:T(8,128)(2,1)S(1)} all-gather(bf16[8,16,512]{2,0,1:T(8,128)(2,1)S(1)} %copy.17), channel_id=1, replica_groups=mesh['y'=4,'zh'=4,'c'=2,'zl'=8,'x'=4] {'y'}, dimensions={0}, use_global_device_ids=true | all-gather | bytes 655360 | tf_op jit(solution)/shard_map/all_gather | solution.py:29
  60.4 1.0 convolution_convert_fusion
  61.4 1.1 copy.18
  62.5 7.7 %all-to-all-start = ((bf16[32,16,512]{2,1,0:T(8,128)(2,1)}), bf16[32,16,512]{2,1,0:T(8,128)(2,1)}, u32[]{:S(2)}, u32[]{:S(2)}) async-start(bf16[32,16,512]{2,1,0:T(8,128)(2,1)} %copy.18), calls=%async_computation | async-start | bytes 1048576 | tf_op jit(solution)/shard_map/all_to_all | solution.py:130
  70.9 0.0 copy-done.4
  70.9 0.0 copy-done.1
  70.9 0.0 copy-start.2
  70.9 0.0 copy-start.3
  70.9 2.0 %gather_fusion = bf16[4,512,512]{2,1,0:T(8,128)(2,1)} fusion(bf16[2,512,512]{2,1,0:T(8,128)(2,1)S(1)} %bitcast.33, s32[1024]{0:T(1024)S(1)} %pad_clamp_fusion), kind=kCustom, calls=%fused_computation | custom fusion | bytes 4194320 | tf_op jit(solution)/shard_map/jit(_take)/gather | solution.py:152
  73.0 0.0 copy-done.2
  73.0 0.0 copy-done.3
  73.0 0.2 select_reduce_fusion
  73.2 21.6 %all-to-all-done = bf16[32,16,512]{2,1,0:T(8,128)(2,1)} async-done(((bf16[32,16,512]{2,1,0:T(8,128)(2,1)}), bf16[32,16,512]{2,1,0:T(8,128)(2,1)}, u32[]{:S(2)}, u32[]{:S(2)}) %all-to-all-start) | async-done | bytes 524320 | tf_op jit(solution)/shard_map/all_to_all | solution.py:130
  94.8 0.0 copy-done
  94.8 4.1 %multiply_reduce_fusion = bf16[512,512]{1,0:T(8,128)(2,1)S(1)} fusion(bf16[4,512,512]{2,1,0:T(8,128)(2,1)} %gather_fusion, f32[4]{0:T(128)S(1)} %compare_select_fusion.2, pred[4]{0:T(512)(128)(4,1)S(1)} %compare_and_fusion, bf16[512,512,1]{1,0,2:T(8,128)(2,1)} %bitcast.9, bf16[1,4,512,512]{3,2,1,0:T(8,128)(2,1)S(1)} %copy-done), kind=kOutput, calls=%fused_computation.1 | convolution fusion | flops 2151415808 | bytes 5242900 | tf_op jit(solution)/shard_map/kij,kjl->kil/dot_general | solution.py:154
  98.9 10.9 %all_to_all.15 = bf16[4,8,16,512]{3,2,1,0:T(8,128)(2,1)S(1)} all-to-all(bf16[4,8,16,512]{3,2,1,0:T(8,128)(2,1)S(1)} %copy.19), channel_id=1, replica_groups=mesh['y'=4,'zh'=4,'c'=2,'zl'=8,'x'=4] {'x'}, dimensions={0} | all-to-all | bytes 1048576 | tf_op jit(solution)/shard_map/all_to_all | solution.py:95
  109.8 0.1 convert_reduce_fusion
  109.9 18.8 %all_to_all.16 = f32[8,16,512]{2,1,0:T(8,128)S(1)} all-to-all(f32[8,16,512]{2,1,0:T(8,128)S(1)} %convert_reduce_fusion), channel_id=1, replica_groups=mesh['y'=4,'zh'=4,'c'=2,'zl'=8,'x'=4] {'zl'}, dimensions={0} | all-to-all | bytes 524288 | tf_op jit(solution)/shard_map/all_to_all | solution.py:97
  128.7 0.6 reduce_sum.39
  (6 shorter events, 0.1 us)
Async XLA Ops:
  0.0 94.8 %copy-start = (bf16[1,4,512,512]{3,2,1,0:T(8,128)(2,1)S(1)}, bf16[1,4,512,512]{3,2,1,0:T(8,128)(2,1)}, u32[]{:S(2)}) copy-start(bf16[1,4,512,512]{3,2,1,0:T(8,128)(2,1)} %param.15) | copy-start | bytes 6291460
  2.2 68.7 %copy-start.4 = (s32[1,4]{1,0:T(1,128)S(1)}, s32[1,4]{1,0:T(1,128)}, u32[]{:S(2)}) copy-start(s32[1,4]{1,0:T(1,128)} %param.12) | copy-start | bytes 52
  2.2 68.7 %copy-start.1 = (bf16[1,2,512,512]{3,2,1,0:T(8,128)(2,1)S(1)}, bf16[1,2,512,512]{3,2,1,0:T(8,128)(2,1)}, u32[]{:S(2)}) copy-start(bf16[1,2,512,512]{3,2,1,0:T(8,128)(2,1)} %param.14) | copy-start | bytes 3145732
  62.5 32.3 %all-to-all-start = ((bf16[32,16,512]{2,1,0:T(8,128)(2,1)}), bf16[32,16,512]{2,1,0:T(8,128)(2,1)}, u32[]{:S(2)}, u32[]{:S(2)}) async-start(bf16[32,16,512]{2,1,0:T(8,128)(2,1)} %copy.18), calls=%async_computation | async-start | bytes 1048576 | tf_op jit(solution)/shard_map/all_to_all | solution.py:130
  70.9 2.1 %copy-start.2 = (f32[64]{0:T(128)S(1)}, f32[64]{0:T(128)}, u32[]{:S(2)}) copy-start(f32[64]{0:T(128)} %param.13) | copy-start | bytes 772
  70.9 2.0 %copy-start.3 = (s32[1,4]{1,0:T(1,128)S(1)}, s32[1,4]{1,0:T(1,128)}, u32[]{:S(2)}) copy-start(s32[1,4]{1,0:T(1,128)} %param.11) | copy-start | bytes 52

commit v7 on v6

--- a/solution.py
+++ b/solution.py
@@ -91,7 +91,7 @@
         t = lax.all_to_all(t, "zl", split_axis=0, concat_axis=0, tiled=True)
         return jnp.sum(t.astype(jnp.float32), axis=0)
     if REDUCE == "h_a2a_xbf":
-        t = total.reshape(8, 4, slab_rows, width).transpose(1, 0, 2, 3).astype(jnp.bfloat16)
+        t = total.reshape(4, 8, slab_rows, width).astype(jnp.bfloat16)
         t = lax.all_to_all(t, "x", split_axis=0, concat_axis=0, tiled=True)
         t = jnp.sum(t.astype(jnp.float32), axis=0)
         t = lax.all_to_all(t, "zl", split_axis=0, concat_axis=0, tiled=True)
@@ -150,6 +150,7 @@
             total = total + weights[k] * jnp.dot(lefts[k], halves[k], preferred_element_type=jnp.float32)
     else:
         lefts = jnp.take(left_ops[0], left_index[0], axis=0)
+        lefts = lefts.reshape(slots, 8, 4, slab_rows, width).transpose(0, 2, 1, 3, 4).reshape(slots, 32 * slab_rows, width)
         halves = jnp.einsum("ij,kjl->kil", block, right_ops[0], preferred_element_type=jnp.float32).astype(jnp.bfloat16)
         prods = jnp.einsum("kij,kjl->kil", lefts, halves, preferred_element_type=jnp.float32)
         total = jnp.sum(weights[:, None, None] * prods, axis=0)

time: 130 us -> 130 us (level)
  waiting for transfers between devices: 21.6 us -> 18.2 us
  other arithmetic: 0.91 us -> 2.76 us
  local copies, waits for them, and re-layouts: 3.27 us -> 4.8 us
    all_to_all x1, waiting for transfers between devices: 21.6 us -> 18.2 us  [body(): lax.all_to_all(outgoing, OPX, split_axis=0, concat_axis=0, tiled=True)]
    transpose x0 -> x1, other arithmetic: none -> 1.85 us  [body(): lefts.reshape(slots, 8, 4, slab_rows, width).transpose(0, 2, 1, 3, 4)]
    transpose x0 -> x1, local copies, waits for them, and re-layouts: none -> 1.56 us  [body(): lefts.reshape(slots, 8, 4, slab_rows, width).transpose(0, 2, 1, 3, 4)]
  transfers between devices with their start and end apart: 1 -> 1, of which waited for: 1 -> 1; matrix products, arithmetic and copies ran while one was open for 2% -> 4% of each run, Pallas kernels for 0% -> 0%
where the time goes in v7:
time: 130 us; the launch traced here: 129 us
  blocking collectives  89.9 us (69%)
  waiting for transfers between devices  18.2 us (14%)
  starting transfers between devices  7.74 us (6%)
  matrix products  5.08 us (4%)
  local copies, waits for them, and re-layouts  4.8 us (4%)
  other arithmetic  2.76 us (2%)
    all_gather x1, blocking collectives, gather_psi(): g = lax.all_gather(g, 'zh', axis=0, tiled=True)  45.1 us
    all_to_all x1, blocking collectives, reduce_out(): t = lax.all_to_all(t, 'zl', split_axis=0, concat_axis=0, tiled=True)  18.8 us
    all_to_all x1, waiting for transfers between devices, body(): lax.all_to_all(outgoing, OPX, split_axis=0, concat_axis=0, tiled=True)  18.2 us
    all_gather x1, blocking collectives, gather_psi(): g = lax.all_gather(g, 'y', axis=0, tiled=True)  13 us
    all_to_all x1, blocking collectives, reduce_out(): t = lax.all_to_all(t, 'x', split_axis=0, concat_axis=0, tiled=True)  10.9 us
    all_to_all x1, starting transfers between devices, body(): lax.all_to_all(outgoing, OPX, split_axis=0, concat_axis=0, tiled=True)  7.74 us
    dot_general x1, matrix products, body(): jnp.einsum('kij,kjl->kil', lefts, halves, preferred_element_type=jnp.floa...  4.07 us
  transfers between devices with their start and end apart: 1, of which 1 were waited for; matrix products, arithmetic and copies ran while one was open for 4% of the time, Pallas kernels for 0%

profile of v7, /device:TPU:8, one launch (start us, length us, event | category | flops | bytes accessed | tf_op | source)
XLA Modules:
  0.0 129.2 jit_solution(12285473570319883696)
XLA Ops:
  0.0 0.0 copy-start
  0.0 2.2 %all_gather.9 = bf16[2,16,512]{2,1,0:T(8,128)(2,1)S(1)} all-gather(bf16[1,16,512]{2,1,0:T(8,128)(2,1)} %param.8), channel_id=1, replica_groups=mesh['y'=4,'zh'=4,'c'=2,'zl'=8,'x'=4] {'c'}, dimensions={0}, use_global_device_ids=true | all-gather | bytes 49152 | tf_op jit(solution)/shard_map/all_gather | solution.py:27
  2.2 45.1 %all_gather.10 = bf16[8,16,512]{2,1,0:T(8,128)(2,1)S(1)} all-gather(bf16[2,16,512]{2,1,0:T(8,128)(2,1)S(1)} %all_gather.9), channel_id=1, replica_groups=mesh['y'=4,'zh'=4,'c'=2,'zl'=8,'x'=4] {'zh'}, dimensions={0}, use_global_device_ids=true | all-gather | bytes 163840 | tf_op jit(solution)/shard_map/all_gather | solution.py:28
  47.3 0.1 copy.18
  47.4 13.0 %all_gather.11 = bf16[32,16,512]{2,0,1:T(8,128)(2,1)S(1)} all-gather(bf16[8,16,512]{2,0,1:T(8,128)(2,1)S(1)} %copy.18), channel_id=1, replica_groups=mesh['y'=4,'zh'=4,'c'=2,'zl'=8,'x'=4] {'y'}, dimensions={0}, use_global_device_ids=true | all-gather | bytes 655360 | tf_op jit(solution)/shard_map/all_gather | solution.py:29
  60.4 1.0 convolution_convert_fusion
  61.4 1.1 copy.19
  62.5 7.7 %all-to-all-start = ((bf16[32,16,512]{2,1,0:T(8,128)(2,1)}), bf16[32,16,512]{2,1,0:T(8,128)(2,1)}, u32[]{:S(2)}, u32[]{:S(2)}) async-start(bf16[32,16,512]{2,1,0:T(8,128)(2,1)} %copy.19), calls=%async_computation | async-start | bytes 1048576 | tf_op jit(solution)/shard_map/all_to_all | solution.py:130
  70.2 0.0 copy-done.2
  70.3 0.0 copy-done.1
  70.3 2.0 %gather_fusion = bf16[4,512,512]{2,1,0:T(8,128)(2,1)} fusion(bf16[2,512,512]{2,1,0:T(8,128)(2,1)S(1)} %bitcast.37, s32[1024]{0:T(1024)S(1)} %pad_clamp_fusion), kind=kCustom, calls=%fused_computation | custom fusion | bytes 4194320 | tf_op jit(solution)/shard_map/jit(_take)/gather | solution.py:152
  72.3 1.9 %select_bitcast_fusion = bf16[4,4,8,16,512]{4,3,1,2,0:T(8,128)(2,1)S(1)} fusion(bf16[4,8,4,16,512]{4,3,2,1,0:T(8,128)(2,1)} %bitcast.36, pred[4]{0:T(512)(128)(4,1)S(1)} %compare_and_fusion), kind=kLoop, calls=%fused_computation.6 | loop fusion | flops 1048576 | bytes 4194308 | tf_op jit(solution)/shard_map/transpose | solution.py:153
  74.2 0.0 copy-start.3
  74.2 0.0 copy-start.4
  74.2 1.6 %copy.17 = bf16[4,4,8,16,512]{4,3,2,1,0:T(8,128)(2,1)} copy(bf16[4,4,8,16,512]{4,3,1,2,0:T(8,128)(2,1)S(1)} %select_bitcast_fusion) | data formatting | bytes 4194304 | tf_op jit(solution)/shard_map/transpose | solution.py:153
  76.4 0.0 copy-done.3
  76.4 0.0 copy-done.4
  76.4 0.2 select_reduce_fusion
  76.6 18.2 %all-to-all-done = bf16[32,16,512]{2,1,0:T(8,128)(2,1)} async-done(((bf16[32,16,512]{2,1,0:T(8,128)(2,1)}), bf16[32,16,512]{2,1,0:T(8,128)(2,1)}, u32[]{:S(2)}, u32[]{:S(2)}) %all-to-all-start) | async-done | bytes 524320 | tf_op jit(solution)/shard_map/all_to_all | solution.py:130
  94.8 4.1 %multiply_reduce_fusion = bf16[512,512]{1,0:T(8,128)(2,1)S(1)} fusion(bf16[4,512,512]{2,1,0:T(8,128)(2,1)} %bitcast.38, f32[4]{0:T(128)S(1)} %compare_select_fusion.2, bf16[512,512,1]{1,0,2:T(8,128)(2,1)} %bitcast.12, bf16[1,4,512,512]{3,2,1,0:T(8,128)(2,1)S(1)} %copy-done), kind=kOutput, calls=%fused_computation.1 | convolution fusion | flops 2150367232 | bytes 5242896 | tf_op jit(solution)/shard_map/kij,kjl->kil/dot_general | solution.py:155
  98.9 10.9 %all_to_all.15 = bf16[4,8,16,512]{3,2,1,0:T(8,128)(2,1)S(1)} all-to-all(bf16[4,8,16,512]{3,2,1,0:T(8,128)(2,1)S(1)} %bitcast.39), channel_id=1, replica_groups=mesh['y'=4,'zh'=4,'c'=2,'zl'=8,'x'=4] {'x'}, dimensions={0} | all-to-all | bytes 1048576 | tf_op jit(solution)/shard_map/all_to_all | solution.py:95
  109.8 0.1 convert_reduce_fusion
  109.8 18.8 %all_to_all.16 = f32[8,16,512]{2,1,0:T(8,128)S(1)} all-to-all(f32[8,16,512]{2,1,0:T(8,128)S(1)} %convert_reduce_fusion), channel_id=1, replica_groups=mesh['y'=4,'zh'=4,'c'=2,'zl'=8,'x'=4] {'zl'}, dimensions={0} | all-to-all | bytes 524288 | tf_op jit(solution)/shard_map/all_to_all | solution.py:97
  128.6 0.6 reduce_sum.39
  (7 shorter events, 0.0 us)
Async XLA Ops:
  0.0 94.8 %copy-start = (bf16[1,4,512,512]{3,2,1,0:T(8,128)(2,1)S(1)}, bf16[1,4,512,512]{3,2,1,0:T(8,128)(2,1)}, u32[]{:S(2)}) copy-start(bf16[1,4,512,512]{3,2,1,0:T(8,128)(2,1)} %param.15) | copy-start | bytes 6291460
  2.2 68.1 %copy-start.2 = (s32[1,4]{1,0:T(1,128)S(1)}, s32[1,4]{1,0:T(1,128)}, u32[]{:S(2)}) copy-start(s32[1,4]{1,0:T(1,128)} %param.12) | copy-start | bytes 52
  2.2 68.1 %copy-start.1 = (bf16[1,2,512,512]{3,2,1,0:T(8,128)(2,1)S(1)}, bf16[1,2,512,512]{3,2,1,0:T(8,128)(2,1)}, u32[]{:S(2)}) copy-start(bf16[1,2,512,512]{3,2,1,0:T(8,128)(2,1)} %param.14) | copy-start | bytes 3145732
  62.5 32.3 %all-to-all-start = ((bf16[32,16,512]{2,1,0:T(8,128)(2,1)}), bf16[32,16,512]{2,1,0:T(8,128)(2,1)}, u32[]{:S(2)}, u32[]{:S(2)}) async-start(bf16[32,16,512]{2,1,0:T(8,128)(2,1)} %copy.19), calls=%async_computation | async-start | bytes 1048576 | tf_op jit(solution)/shard_map/all_to_all | solution.py:130
  74.2 2.2 %copy-start.3 = (f32[64]{0:T(128)S(1)}, f32[64]{0:T(128)}, u32[]{:S(2)}) copy-start(f32[64]{0:T(128)} %param.13) | copy-start | bytes 772
  74.2 2.2 %copy-start.4 = (s32[1,4]{1,0:T(1,128)S(1)}, s32[1,4]{1,0:T(1,128)}, u32[]{:S(2)}) copy-start(s32[1,4]{1,0:T(1,128)} %param.11) | copy-start | bytes 52
